TPU v7x, 32 devices: a whole 2x2x4 slice. The times are simulated.
32 devices in a mesh: hyper: 2 (over x), row: 16 (over z, y, core).
Axes of the slice: x: 2, y: 2, z: 4, core: 2. Of those that a mesh axis runs over, the one named last changes fastest.
Arguments:
- carried_block: float32 [8192, 4096], P(('hyper', 'row')), parts along dimension 0, as said below
- coupling_values: float32 [8192, 256], P(('hyper', 'row')), parts along dimension 0, may hold values from -0.15 to 0.15
- block_cols: int32 [128, 8], P('row'), may hold values from 0 to 127, as said below
- next_block: float32 [8192, 4096], P(('hyper', 'row')), parts along dimension 0, as said below
- fixed_rows: float32 [32, 4096], P('hyper', 'row'), parts along dimension 0, may hold values from -0.1875 to 0.1875
- fixed_next: float32 [32, 4096], P('hyper', 'row'), parts along dimension 0, may hold values from -6 to 6
- tip_block: float32 [32, 16], P('hyper'), parts along dimension 0, as said below
Outputs:
- factor_state: float32 [8192, 4096], P(('hyper', 'row')), parts along dimension 0
- coupling_factor: float32 [8192, 4096], P(('hyper', 'row')), parts along dimension 0
- carried_next: float32 [8192, 4096], P(('hyper', 'row')), parts along dimension 0
- fixed_factor: float32 [32, 4096], P('hyper', 'row'), parts along dimension 0
- fixed_carried: float32 [32, 4096], P('hyper', 'row'), parts along dimension 0
- tip_next: float32 [32, 16], P('hyper'), parts along dimension 0
There are 2 independent parts, one for each index of `hyper`. A program takes and returns all parts, laid end to end along the dimension named above; an argument that names none is the same for every part. Nothing has to cross between parts.
Inputs may be any that keep to these rules, and one draw needn't show every extreme that they name: `block_cols`: row r lists 8 distinct block columns; the first is r itself, the others lie within 32 blocks of r, cyclically. `carried_block`: symmetric positive definite. `next_block`: symmetric positive definite. `tip_block`: Symmetric.
All inputs are finite; a program needn't handle non-finite values.
Results may differ from a plain program's by a relative error of at most 0.0001.
Values sent between devices are 32-bit elements; how exact they have to be, the bound alone decides.
No kernel may reach another device: no remote copies, remote signals or barrier semaphores. Data moves between devices by JAX's collectives and lax.ppermute only.
A program may use at most 128 MiB of HBM per device.

v0:
```python
import jax
import jax.numpy as jnp
from jax import lax
from jax.sharding import PartitionSpec as P

PANELS = 4
NB = 128


def broadcast(block, axis, owner):
    block = jnp.where(lax.axis_index(axis) == owner, block, jnp.zeros_like(block))
    return lax.psum(block, axis)


def matmul(left, right):
    return jnp.dot(left, right, precision=lax.Precision.HIGHEST, preferred_element_type=jnp.float32)


def assemble(block_cols, values):
    block_rows, nonzero = block_cols.shape
    width = values.shape[1] // nonzero
    columns = jnp.arange(NB, dtype=jnp.int32)
    onehot = (block_cols[:, :, None] == columns[None, None, :]).astype(values.dtype)
    shaped = values.reshape(block_rows, width, nonzero, width)
    dense = jnp.einsum("bsn,btsc->btnc", onehot, shaped, precision=lax.Precision.HIGHEST)
    return dense.reshape(block_rows * width, NB * width)


def lower_solve(tile, right):
    return jax.scipy.linalg.solve_triangular(tile, right, lower=True)


def on_device(
    carried_block, coupling_values, block_cols, next_block, fixed_rows, fixed_next, tip_block
):
    local_rows = carried_block.shape[0]
    own_index = lax.axis_index("row")
    column = jnp.arange(carried_block.shape[1], dtype=jnp.int32)
    identity_tile = jnp.eye(local_rows, dtype=jnp.float32)
    coupled_start = assemble(block_cols, coupling_values)

    def step(panel, carry_in):
        state, coupled, carried, fixed, fixed_carry, partial_value = carry_in
        begin = panel * local_rows
        own_cols = lax.dynamic_slice_in_dim(state, begin, local_rows, 1)
        coupled_cols = lax.dynamic_slice_in_dim(coupled, begin, local_rows, 1)
        is_owner = own_index == panel
        tile_input = jnp.where(is_owner, own_cols, identity_tile)
        own_tile = jnp.linalg.cholesky(tile_input)
        own_fixed = lower_solve(own_tile, fixed.T).T
        tile, fixed_panel = (broadcast(own_tile, "row", panel), broadcast(own_fixed, "row", panel))
        solved_mine = lower_solve(tile, own_cols.T)
        solved_mine = jnp.where(own_index > panel, solved_mine, jnp.where(is_owner, tile.T, 0.0))
        coupled_mine = lower_solve(tile, coupled_cols.T)
        lower_rows = solved_mine.T
        coupled_rows = coupled_mine.T
        piece = lax.all_gather(jnp.stack([solved_mine, coupled_mine]), "row", axis=2, tiled=True)
        updates = jnp.stack(
            [
                matmul(lower_rows, piece[0]),
                matmul(coupled_rows, piece[0]),
                matmul(coupled_rows, piece[1]),
            ]
        )
        state = state - updates[0]
        state = lax.dynamic_update_slice_in_dim(state, lower_rows, begin, 1)
        state = jnp.where(is_owner & (column[None, :] >= begin + local_rows), 0.0, state)
        coupled = coupled - updates[1]
        coupled = lax.dynamic_update_slice_in_dim(coupled, coupled_rows, begin, 1)
        carried = carried - updates[2]
        fixed = fixed - matmul(fixed_panel, solved_mine)
        fixed = jnp.where(is_owner, fixed_panel, fixed)
        fixed_carry = fixed_carry - matmul(fixed_panel, coupled_mine)
        square = matmul(fixed_panel, fixed_panel.T)
        partial_value = partial_value + jnp.where(is_owner, square, 0.0)
        return (state, coupled, carried, fixed, fixed_carry, partial_value)

    start_state = (
        carried_block,
        coupled_start,
        next_block,
        fixed_rows,
        fixed_next,
        jnp.zeros_like(tip_block),
    )
    state, coupled, carried, fixed, fixed_carry, partial_value = lax.fori_loop(
        0, PANELS, step, start_state
    )
    tip_next = tip_block - lax.psum(partial_value, "row")
    return (state, coupled, carried, fixed, fixed_carry, tip_next)


def solution(mesh):
    return jax.shard_map(
        on_device,
        mesh=mesh,
        in_specs=(
            P(("hyper", "row"), None),
            P(("hyper", "row"), None),
            P("row", None),
            P(("hyper", "row"), None),
            P("hyper", "row"),
            P("hyper", "row"),
            P("hyper", None),
        ),
        out_specs=(
            P(("hyper", "row"), None),
            P(("hyper", "row"), None),
            P(("hyper", "row"), None),
            P("hyper", "row"),
            P("hyper", "row"),
            P("hyper", None),
        ),
        check_vma=False,
    )
```

profile of v0, /device:TPU:0, one launch (start us, length us, event | category | flops | bytes accessed | tf_op | source)
XLA Modules:
  0.0 1204.6 jit_solution(10268459732138265144)
XLA Ops:
  17.2 10.4 copy.37
  27.7 13.0 %reshape.75 = f32[256,4096]{1,0:T(8,128)} reshape(f32[8,32,128,32]{3,2,1,0:T(8,128)} %copy.37) | data formatting | bytes 8388608 | tf_op jit(solution)/shard_map/reshape | solution.py:26
  46.3 1115.2 %while.34 = (s32[]{:T(128)}, f32[256,4096]{0,1:T(8,128)}, f32[256,4096]{1,0:T(8,128)}, f32[256,4096]{1,0:T(8,128)}, f32[16,256]{1,0:T(8,128)S(1)}, /*index=5*/f3...) while((s32[]{:T(128)}, f32[256,4096]{0,1:T(8,128)}, ...), condition=%wide.region_7.9_spmd.clone, body=%wide.region_0.8_spmd.clone.sunk | while | flops 10057272320 | bytes 141284144 | solution.py:86
  47.8 11.7 cholesky.232
  59.5 9.8 custom-call.43
  70.0 11.7 cholesky.234
  85.6 90.5 %all-reduce.3.cloned.1.call-done = f32[256,256]{0,1:T(8,128)} async-done(((f32[256,256]{0,1:T(8,128)}), f32[256,256]{0,1:T(8,128)}) %all-reduce.3.cloned.1.call-update) | async-done | bytes 262160 | tf_op jit(solution)/shard_map/while/body/eval_jaxpr/psum | solution.py:12
  181.5 19.7 %custom-call.44 = f32[2,128,128]{1,2,0:T(8,128)S(1)} custom-call(f32[2,128,128]{2,1,0:T(8,128)S(1)} %get-tuple-element.487), custom_call_target="InvertDiagBlocksLowerTriangular" | custom-call | tf_op jit(solution)/shard_map/while/body/eval_jaxpr/jit(_solve_triangular)/triangular_solve | solution.py:30
  214.0 19.7 %custom-call.45 = f32[2,128,128]{1,2,0:T(8,128)S(1)} custom-call(f32[2,128,128]{2,1,0:T(8,128)S(1)} %get-tuple-element.491), custom_call_target="InvertDiagBlocksLowerTriangular" | custom-call | tf_op jit(solution)/shard_map/while/body/eval_jaxpr/jit(_solve_triangular)/triangular_solve | solution.py:30
  234.2 61.5 %psum.35 = f32[16,256]{1,0:T(8,128)S(1)} all-reduce(f32[16,256]{1,0:T(8,128)S(1)} %fusion.126), channel_id=1, replica_groups=mesh['hyper'=2,'row'=16] {'row'}, use_global_device_ids=true, to_apply=%region_6.7 | all-reduce | flops 4096 | bytes 32768 | tf_op jit(solution)/shard_map/while/body/eval_jaxpr/psum | solution.py:12
  330.7 11.7 cholesky.232
  342.4 9.8 custom-call.43
  352.9 11.7 cholesky.234
  368.5 85.0 %all-reduce.3.cloned.1.call-done = f32[256,256]{0,1:T(8,128)} async-done(((f32[256,256]{0,1:T(8,128)}), f32[256,256]{0,1:T(8,128)}) %all-reduce.3.cloned.1.call-update) | async-done | bytes 262160 | tf_op jit(solution)/shard_map/while/body/eval_jaxpr/psum | solution.py:12
  458.8 19.7 %custom-call.44 = f32[2,128,128]{1,2,0:T(8,128)S(1)} custom-call(f32[2,128,128]{2,1,0:T(8,128)S(1)} %get-tuple-element.487), custom_call_target="InvertDiagBlocksLowerTriangular" | custom-call | tf_op jit(solution)/shard_map/while/body/eval_jaxpr/jit(_solve_triangular)/triangular_solve | solution.py:30
  491.4 19.7 %custom-call.45 = f32[2,128,128]{1,2,0:T(8,128)S(1)} custom-call(f32[2,128,128]{2,1,0:T(8,128)S(1)} %get-tuple-element.491), custom_call_target="InvertDiagBlocksLowerTriangular" | custom-call | tf_op jit(solution)/shard_map/while/body/eval_jaxpr/jit(_solve_triangular)/triangular_solve | solution.py:30
  511.6 61.5 %psum.35 = f32[16,256]{1,0:T(8,128)S(1)} all-reduce(f32[16,256]{1,0:T(8,128)S(1)} %fusion.126), channel_id=1, replica_groups=mesh['hyper'=2,'row'=16] {'row'}, use_global_device_ids=true, to_apply=%region_6.7 | all-reduce | flops 4096 | bytes 32768 | tf_op jit(solution)/shard_map/while/body/eval_jaxpr/psum | solution.py:12
  608.0 11.7 cholesky.232
  619.8 9.8 custom-call.43
  630.3 11.7 cholesky.234
  645.9 85.0 %all-reduce.3.cloned.1.call-done = f32[256,256]{0,1:T(8,128)} async-done(((f32[256,256]{0,1:T(8,128)}), f32[256,256]{0,1:T(8,128)}) %all-reduce.3.cloned.1.call-update) | async-done | bytes 262160 | tf_op jit(solution)/shard_map/while/body/eval_jaxpr/psum | solution.py:12
  736.2 19.7 %custom-call.44 = f32[2,128,128]{1,2,0:T(8,128)S(1)} custom-call(f32[2,128,128]{2,1,0:T(8,128)S(1)} %get-tuple-element.487), custom_call_target="InvertDiagBlocksLowerTriangular" | custom-call | tf_op jit(solution)/shard_map/while/body/eval_jaxpr/jit(_solve_triangular)/triangular_solve | solution.py:30
  768.7 19.7 %custom-call.45 = f32[2,128,128]{1,2,0:T(8,128)S(1)} custom-call(f32[2,128,128]{2,1,0:T(8,128)S(1)} %get-tuple-element.491), custom_call_target="InvertDiagBlocksLowerTriangular" | custom-call | tf_op jit(solution)/shard_map/while/body/eval_jaxpr/jit(_solve_triangular)/triangular_solve | solution.py:30
  788.9 61.5 %psum.35 = f32[16,256]{1,0:T(8,128)S(1)} all-reduce(f32[16,256]{1,0:T(8,128)S(1)} %fusion.126), channel_id=1, replica_groups=mesh['hyper'=2,'row'=16] {'row'}, use_global_device_ids=true, to_apply=%region_6.7 | all-reduce | flops 4096 | bytes 32768 | tf_op jit(solution)/shard_map/while/body/eval_jaxpr/psum | solution.py:12
  885.4 11.7 cholesky.232
  897.1 9.8 custom-call.43
  907.6 11.7 cholesky.234
  923.2 85.0 %all-reduce.3.cloned.1.call-done = f32[256,256]{0,1:T(8,128)} async-done(((f32[256,256]{0,1:T(8,128)}), f32[256,256]{0,1:T(8,128)}) %all-reduce.3.cloned.1.call-update) | async-done | bytes 262160 | tf_op jit(solution)/shard_map/while/body/eval_jaxpr/psum | solution.py:12
  1013.5 19.7 %custom-call.44 = f32[2,128,128]{1,2,0:T(8,128)S(1)} custom-call(f32[2,128,128]{2,1,0:T(8,128)S(1)} %get-tuple-element.487), custom_call_target="InvertDiagBlocksLowerTriangular" | custom-call | tf_op jit(solution)/shard_map/while/body/eval_jaxpr/jit(_solve_triangular)/triangular_solve | solution.py:30
  1046.0 19.7 %custom-call.45 = f32[2,128,128]{1,2,0:T(8,128)S(1)} custom-call(f32[2,128,128]{2,1,0:T(8,128)S(1)} %get-tuple-element.491), custom_call_target="InvertDiagBlocksLowerTriangular" | custom-call | tf_op jit(solution)/shard_map/while/body/eval_jaxpr/jit(_solve_triangular)/triangular_solve | solution.py:30
  1066.2 61.5 %psum.35 = f32[16,256]{1,0:T(8,128)S(1)} all-reduce(f32[16,256]{1,0:T(8,128)S(1)} %fusion.126), channel_id=1, replica_groups=mesh['hyper'=2,'row'=16] {'row'}, use_global_device_ids=true, to_apply=%region_6.7 | all-reduce | flops 4096 | bytes 32768 | tf_op jit(solution)/shard_map/while/body/eval_jaxpr/psum | solution.py:12
  1167.1 30.0 %psum.29 = f32[16,16]{1,0:T(8,128)S(1)} all-reduce(f32[16,16]{1,0:T(8,128)S(1)} %get-tuple-element.186), channel_id=1, replica_groups=mesh['hyper'=2,'row'=16] {'row'}, use_global_device_ids=true, to_apply=%region_8.10 | all-reduce | flops 256 | bytes 2048 | tf_op jit(solution)/shard_map/psum | solution.py:89
  (349 shorter events, 282.0 us)
Async XLA Ops:
  7.2 4.7 copy-start.7
  7.2 5.0 copy-start.9
  40.7 5.6 copy-start.4
  40.7 5.6 copy-start.6
  46.5 129.6 %all-reduce.3.cloned.1.call-start = ((), (), s32[]{:S(2)}) async-start(), calls=%async_computation | async-start | bytes 524288 | tf_op jit(solution)/shard_map/while/body/eval_jaxpr/psum | solution.py:12
  84.6 212.0 %all-gather.2.cloned.1.call-start = ((), (), s32[]{:S(2)}) async-start(), calls=%async_computation.1 | async-start | bytes 8912896 | tf_op jit(solution)/shard_map/while/body/eval_jaxpr/all_gather | solution.py:57
  176.1 27.0 %copy-start.2 = (f32[256,256]{0,1:T(8,128)S(1)}, f32[256,256]{0,1:T(8,128)}, u32[]{:S(2)}) copy-start(f32[256,256]{0,1:T(8,128)} %all-reduce.3.cloned.1.call-done) | copy-start | bytes 786436 | tf_op jit(solution)/shard_map/while
  312.1 9.7 copy-start
  327.5 2.0 copy-start.1
  329.5 124.0 %all-reduce.3.cloned.1.call-start = ((), (), s32[]{:S(2)}) async-start(), calls=%async_computation | async-start | bytes 524288 | tf_op jit(solution)/shard_map/while/body/eval_jaxpr/psum | solution.py:12
  367.4 206.5 %all-gather.2.cloned.1.call-start = ((), (), s32[]{:S(2)}) async-start(), calls=%async_computation.1 | async-start | bytes 8912896 | tf_op jit(solution)/shard_map/while/body/eval_jaxpr/all_gather | solution.py:57
  453.5 27.0 %copy-start.2 = (f32[256,256]{0,1:T(8,128)S(1)}, f32[256,256]{0,1:T(8,128)}, u32[]{:S(2)}) copy-start(f32[256,256]{0,1:T(8,128)} %all-reduce.3.cloned.1.call-done) | copy-start | bytes 786436 | tf_op jit(solution)/shard_map/while
  589.4 9.7 copy-start
  604.8 2.0 copy-start.1
  606.8 124.0 %all-reduce.3.cloned.1.call-start = ((), (), s32[]{:S(2)}) async-start(), calls=%async_computation | async-start | bytes 524288 | tf_op jit(solution)/shard_map/while/body/eval_jaxpr/psum | solution.py:12
  644.8 206.5 %all-gather.2.cloned.1.call-start = ((), (), s32[]{:S(2)}) async-start(), calls=%async_computation.1 | async-start | bytes 8912896 | tf_op jit(solution)/shard_map/while/body/eval_jaxpr/all_gather | solution.py:57
  730.8 27.0 %copy-start.2 = (f32[256,256]{0,1:T(8,128)S(1)}, f32[256,256]{0,1:T(8,128)}, u32[]{:S(2)}) copy-start(f32[256,256]{0,1:T(8,128)} %all-reduce.3.cloned.1.call-done) | copy-start | bytes 786436 | tf_op jit(solution)/shard_map/while
  866.8 9.7 copy-start
  882.2 2.0 copy-start.1
  884.2 124.0 %all-reduce.3.cloned.1.call-start = ((), (), s32[]{:S(2)}) async-start(), calls=%async_computation | async-start | bytes 524288 | tf_op jit(solution)/shard_map/while/body/eval_jaxpr/psum | solution.py:12
  922.1 206.5 %all-gather.2.cloned.1.call-start = ((), (), s32[]{:S(2)}) async-start(), calls=%async_computation.1 | async-start | bytes 8912896 | tf_op jit(solution)/shard_map/while/body/eval_jaxpr/all_gather | solution.py:57
  1008.2 27.0 %copy-start.2 = (f32[256,256]{0,1:T(8,128)S(1)}, f32[256,256]{0,1:T(8,128)}, u32[]{:S(2)}) copy-start(f32[256,256]{0,1:T(8,128)} %all-reduce.3.cloned.1.call-done) | copy-start | bytes 786436 | tf_op jit(solution)/shard_map/while
  1144.1 9.7 copy-start
  1159.5 2.0 copy-start.1
  1161.5 5.6 copy-start.3
  1161.5 5.6 copy-start.5
  1161.5 35.6 %copy-start.8 = (f32[16,16]{1,0:T(8,128)S(1)}, f32[16,16]{1,0:T(8,128)}, u32[]{:S(2)}) copy-start(f32[16,16]{1,0:T(8,128)} %param.17) | copy-start | bytes 3076
Sparse Core Ops, SparseCore 0:
  84.7 91.3 all-reduce.2
  204.2 79.6 all-gather.1
  367.6 85.8 all-reduce.2
  481.6 79.6 all-gather.1
  644.9 85.8 all-reduce.2
  758.9 79.6 all-gather.1
  922.3 85.8 all-reduce.2
  1036.3 79.6 all-gather.1
where the time goes:
time: 1210 us; the launch traced here: 1200 us
  waiting for transfers between devices  346 us (29%)
  other arithmetic  318 us (26%)
  blocking collectives  276 us (23%)
  local copies, waits for them, and re-layouts  136 us (11%)
  matrix products  108 us (9%)
  between operations  14.1 us (1%)
    psum x4, waiting for transfers between devices, broadcast(): return lax.psum(block, axis)  345 us
    psum x4, blocking collectives, broadcast(): return lax.psum(block, axis)  246 us
    another operation x20, other arithmetic, lower_solve(): return jax.scipy.linalg.solve_triangular(tile, right, lower=True)  165 us
    another operation x24, other arithmetic, step(): own_tile = jnp.linalg.cholesky(tile_input)  136 us
    dot_general x24, matrix products, matmul(): jnp.dot(left, right, precision=lax.Precision.HIGHEST, preferred_element_t...  90.8 us
    while x32, local copies, waits for them, and re-layouts  52.9 us
    psum x1, blocking collectives, on_device(): tip_next = tip_block - lax.psum(partial_value, 'row')  30 us
  transfers between devices with their start and end apart: 8, of which 4 were waited for; matrix products, arithmetic and copies ran while one was open for 11% of the time, Pallas kernels for 0%

commit v1 on v0

--- a/solution.py
+++ b/solution.py
@@ -86,7 +86,7 @@
     state, coupled, carried, fixed, fixed_carry, partial_value = lax.fori_loop(
         0, PANELS, step, start_state
     )
-    tip_next = tip_block - lax.psum(partial_value, "row")
+    tip_next = tip_block - jnp.sum(lax.all_gather(partial_value, "row"), axis=0)
     return (state, coupled, carried, fixed, fixed_carry, tip_next)
 
 

time: 1210 us -> 1190 us (0.983)
  blocking collectives: 276 us -> 263 us
    psum x1 -> x0, blocking collectives: 30 us -> none  [on_device(): tip_next = tip_block - lax.psum(partial_value, 'row')]
    all_gather x0 -> x1, blocking collectives: none -> 17.5 us  [on_device(): tip_next = tip_block - jnp.sum(lax.all_gather(partial_value, 'row'), axis=0)]
where the time goes in v1:
time: 1190 us
  waiting for transfers between devices  346 us (29%)
  other arithmetic  318 us (27%)
  blocking collectives  263 us (22%)
  local copies, waits for them, and re-layouts  136 us (11%)
  matrix products  108 us (9%)
  between operations  14 us (1%)
    psum x4, waiting for transfers between devices, broadcast(): return lax.psum(block, axis)  345 us
    psum x4, blocking collectives, broadcast(): return lax.psum(block, axis)  246 us
    another operation x20, other arithmetic, lower_solve(): return jax.scipy.linalg.solve_triangular(tile, right, lower=True)  165 us
    another operation x24, other arithmetic, step(): own_tile = jnp.linalg.cholesky(tile_input)  136 us
    dot_general x24, matrix products, matmul(): jnp.dot(left, right, precision=lax.Precision.HIGHEST, preferred_element_t...  90.8 us
    while x32, local copies, waits for them, and re-layouts  52.9 us
  transfers between devices with their start and end apart: 8, of which 4 were waited for; matrix products, arithmetic and copies ran while one was open for 11% of the time, Pallas kernels for 0%

profile of v1, /device:TPU:0, one launch (start us, length us, event | category | flops | bytes accessed | tf_op | source)
XLA Modules:
  0.0 1192.1 jit_solution(14355801312296099061)
XLA Ops:
  17.2 10.4 copy.37
  27.7 13.0 %reshape.75 = f32[256,4096]{1,0:T(8,128)} reshape(f32[8,32,128,32]{3,2,1,0:T(8,128)} %copy.37) | data formatting | bytes 8388608 | tf_op jit(solution)/shard_map/reshape | solution.py:26
  46.3 1115.2 %while.34 = (s32[]{:T(128)}, f32[256,4096]{0,1:T(8,128)}, f32[256,4096]{1,0:T(8,128)}, f32[256,4096]{1,0:T(8,128)}, f32[16,256]{1,0:T(8,128)S(1)}, /*index=5*/f3...) while((s32[]{:T(128)}, f32[256,4096]{0,1:T(8,128)}, ...), condition=%wide.region_7.9_spmd.clone, body=%wide.region_0.8_spmd.clone.sunk | while | flops 10057272320 | bytes 141284144 | solution.py:86
  47.8 11.7 cholesky.232
  59.5 9.8 custom-call.43
  70.0 11.7 cholesky.234
  85.6 90.5 %all-reduce.3.cloned.1.call-done = f32[256,256]{0,1:T(8,128)} async-done(((f32[256,256]{0,1:T(8,128)}), f32[256,256]{0,1:T(8,128)}) %all-reduce.3.cloned.1.call-update) | async-done | bytes 262160 | tf_op jit(solution)/shard_map/while/body/eval_jaxpr/psum | solution.py:12
  181.5 19.7 %custom-call.44 = f32[2,128,128]{1,2,0:T(8,128)S(1)} custom-call(f32[2,128,128]{2,1,0:T(8,128)S(1)} %get-tuple-element.487), custom_call_target="InvertDiagBlocksLowerTriangular" | custom-call | tf_op jit(solution)/shard_map/while/body/eval_jaxpr/jit(_solve_triangular)/triangular_solve | solution.py:30
  214.0 19.7 %custom-call.45 = f32[2,128,128]{1,2,0:T(8,128)S(1)} custom-call(f32[2,128,128]{2,1,0:T(8,128)S(1)} %get-tuple-element.491), custom_call_target="InvertDiagBlocksLowerTriangular" | custom-call | tf_op jit(solution)/shard_map/while/body/eval_jaxpr/jit(_solve_triangular)/triangular_solve | solution.py:30
  234.2 61.5 %psum.27 = f32[16,256]{1,0:T(8,128)S(1)} all-reduce(f32[16,256]{1,0:T(8,128)S(1)} %fusion.126), channel_id=1, replica_groups=mesh['hyper'=2,'row'=16] {'row'}, use_global_device_ids=true, to_apply=%region_6.7 | all-reduce | flops 4096 | bytes 32768 | tf_op jit(solution)/shard_map/while/body/eval_jaxpr/psum | solution.py:12
  330.7 11.7 cholesky.232
  342.4 9.8 custom-call.43
  352.9 11.7 cholesky.234
  368.5 85.0 %all-reduce.3.cloned.1.call-done = f32[256,256]{0,1:T(8,128)} async-done(((f32[256,256]{0,1:T(8,128)}), f32[256,256]{0,1:T(8,128)}) %all-reduce.3.cloned.1.call-update) | async-done | bytes 262160 | tf_op jit(solution)/shard_map/while/body/eval_jaxpr/psum | solution.py:12
  458.8 19.7 %custom-call.44 = f32[2,128,128]{1,2,0:T(8,128)S(1)} custom-call(f32[2,128,128]{2,1,0:T(8,128)S(1)} %get-tuple-element.487), custom_call_target="InvertDiagBlocksLowerTriangular" | custom-call | tf_op jit(solution)/shard_map/while/body/eval_jaxpr/jit(_solve_triangular)/triangular_solve | solution.py:30
  491.4 19.7 %custom-call.45 = f32[2,128,128]{1,2,0:T(8,128)S(1)} custom-call(f32[2,128,128]{2,1,0:T(8,128)S(1)} %get-tuple-element.491), custom_call_target="InvertDiagBlocksLowerTriangular" | custom-call | tf_op jit(solution)/shard_map/while/body/eval_jaxpr/jit(_solve_triangular)/triangular_solve | solution.py:30
  511.6 61.5 %psum.27 = f32[16,256]{1,0:T(8,128)S(1)} all-reduce(f32[16,256]{1,0:T(8,128)S(1)} %fusion.126), channel_id=1, replica_groups=mesh['hyper'=2,'row'=16] {'row'}, use_global_device_ids=true, to_apply=%region_6.7 | all-reduce | flops 4096 | bytes 32768 | tf_op jit(solution)/shard_map/while/body/eval_jaxpr/psum | solution.py:12
  608.0 11.7 cholesky.232
  619.8 9.8 custom-call.43
  630.3 11.7 cholesky.234
  645.9 85.0 %all-reduce.3.cloned.1.call-done = f32[256,256]{0,1:T(8,128)} async-done(((f32[256,256]{0,1:T(8,128)}), f32[256,256]{0,1:T(8,128)}) %all-reduce.3.cloned.1.call-update) | async-done | bytes 262160 | tf_op jit(solution)/shard_map/while/body/eval_jaxpr/psum | solution.py:12
  736.2 19.7 %custom-call.44 = f32[2,128,128]{1,2,0:T(8,128)S(1)} custom-call(f32[2,128,128]{2,1,0:T(8,128)S(1)} %get-tuple-element.487), custom_call_target="InvertDiagBlocksLowerTriangular" | custom-call | tf_op jit(solution)/shard_map/while/body/eval_jaxpr/jit(_solve_triangular)/triangular_solve | solution.py:30
  768.7 19.7 %custom-call.45 = f32[2,128,128]{1,2,0:T(8,128)S(1)} custom-call(f32[2,128,128]{2,1,0:T(8,128)S(1)} %get-tuple-element.491), custom_call_target="InvertDiagBlocksLowerTriangular" | custom-call | tf_op jit(solution)/shard_map/while/body/eval_jaxpr/jit(_solve_triangular)/triangular_solve | solution.py:30
  788.9 61.5 %psum.27 = f32[16,256]{1,0:T(8,128)S(1)} all-reduce(f32[16,256]{1,0:T(8,128)S(1)} %fusion.126), channel_id=1, replica_groups=mesh['hyper'=2,'row'=16] {'row'}, use_global_device_ids=true, to_apply=%region_6.7 | all-reduce | flops 4096 | bytes 32768 | tf_op jit(solution)/shard_map/while/body/eval_jaxpr/psum | solution.py:12
  885.4 11.7 cholesky.232
  897.1 9.8 custom-call.43
  907.6 11.7 cholesky.234
  923.2 85.0 %all-reduce.3.cloned.1.call-done = f32[256,256]{0,1:T(8,128)} async-done(((f32[256,256]{0,1:T(8,128)}), f32[256,256]{0,1:T(8,128)}) %all-reduce.3.cloned.1.call-update) | async-done | bytes 262160 | tf_op jit(solution)/shard_map/while/body/eval_jaxpr/psum | solution.py:12
  1013.5 19.7 %custom-call.44 = f32[2,128,128]{1,2,0:T(8,128)S(1)} custom-call(f32[2,128,128]{2,1,0:T(8,128)S(1)} %get-tuple-element.487), custom_call_target="InvertDiagBlocksLowerTriangular" | custom-call | tf_op jit(solution)/shard_map/while/body/eval_jaxpr/jit(_solve_triangular)/triangular_solve | solution.py:30
  1046.0 19.7 %custom-call.45 = f32[2,128,128]{1,2,0:T(8,128)S(1)} custom-call(f32[2,128,128]{2,1,0:T(8,128)S(1)} %get-tuple-element.491), custom_call_target="InvertDiagBlocksLowerTriangular" | custom-call | tf_op jit(solution)/shard_map/while/body/eval_jaxpr/jit(_solve_triangular)/triangular_solve | solution.py:30
  1066.2 61.5 %psum.27 = f32[16,256]{1,0:T(8,128)S(1)} all-reduce(f32[16,256]{1,0:T(8,128)S(1)} %fusion.126), channel_id=1, replica_groups=mesh['hyper'=2,'row'=16] {'row'}, use_global_device_ids=true, to_apply=%region_6.7 | all-reduce | flops 4096 | bytes 32768 | tf_op jit(solution)/shard_map/while/body/eval_jaxpr/psum | solution.py:12
  1167.1 17.5 %all-gather = f32[256,16]{1,0:T(8,128)S(1)} all-gather(f32[16,16]{1,0:T(8,128)S(1)} %get-tuple-element.186), channel_id=2, replica_groups=mesh['hyper'=2,'row'=16] {'row'}, dimensions={0}, use_global_device_ids=true | all-gather | bytes 17408 | tf_op jit(solution)/shard_map/all_gather | solution.py:89
  (350 shorter events, 282.0 us)
Async XLA Ops:
  7.2 4.7 copy-start.7
  7.2 5.0 copy-start.9
  40.7 5.6 copy-start.4
  40.7 5.6 copy-start.6
  46.5 129.6 %all-reduce.3.cloned.1.call-start = ((), (), s32[]{:S(2)}) async-start(), calls=%async_computation | async-start | bytes 524288 | tf_op jit(solution)/shard_map/while/body/eval_jaxpr/psum | solution.py:12
  84.6 212.0 %all-gather.3.cloned.1.call-start = ((), (), s32[]{:S(2)}) async-start(), calls=%async_computation.1 | async-start | bytes 8912896 | tf_op jit(solution)/shard_map/while/body/eval_jaxpr/all_gather | solution.py:57
  176.1 27.0 %copy-start.2 = (f32[256,256]{0,1:T(8,128)S(1)}, f32[256,256]{0,1:T(8,128)}, u32[]{:S(2)}) copy-start(f32[256,256]{0,1:T(8,128)} %all-reduce.3.cloned.1.call-done) | copy-start | bytes 786436 | tf_op jit(solution)/shard_map/while
  312.1 9.7 copy-start
  327.5 2.0 copy-start.1
  329.5 124.0 %all-reduce.3.cloned.1.call-start = ((), (), s32[]{:S(2)}) async-start(), calls=%async_computation | async-start | bytes 524288 | tf_op jit(solution)/shard_map/while/body/eval_jaxpr/psum | solution.py:12
  367.4 206.5 %all-gather.3.cloned.1.call-start = ((), (), s32[]{:S(2)}) async-start(), calls=%async_computation.1 | async-start | bytes 8912896 | tf_op jit(solution)/shard_map/while/body/eval_jaxpr/all_gather | solution.py:57
  453.5 27.0 %copy-start.2 = (f32[256,256]{0,1:T(8,128)S(1)}, f32[256,256]{0,1:T(8,128)}, u32[]{:S(2)}) copy-start(f32[256,256]{0,1:T(8,128)} %all-reduce.3.cloned.1.call-done) | copy-start | bytes 786436 | tf_op jit(solution)/shard_map/while
  589.4 9.7 copy-start
  604.8 2.0 copy-start.1
  606.8 124.0 %all-reduce.3.cloned.1.call-start = ((), (), s32[]{:S(2)}) async-start(), calls=%async_computation | async-start | bytes 524288 | tf_op jit(solution)/shard_map/while/body/eval_jaxpr/psum | solution.py:12
  644.8 206.5 %all-gather.3.cloned.1.call-start = ((), (), s32[]{:S(2)}) async-start(), calls=%async_computation.1 | async-start | bytes 8912896 | tf_op jit(solution)/shard_map/while/body/eval_jaxpr/all_gather | solution.py:57
  730.8 27.0 %copy-start.2 = (f32[256,256]{0,1:T(8,128)S(1)}, f32[256,256]{0,1:T(8,128)}, u32[]{:S(2)}) copy-start(f32[256,256]{0,1:T(8,128)} %all-reduce.3.cloned.1.call-done) | copy-start | bytes 786436 | tf_op jit(solution)/shard_map/while
  866.8 9.7 copy-start
  882.2 2.0 copy-start.1
  884.2 124.0 %all-reduce.3.cloned.1.call-start = ((), (), s32[]{:S(2)}) async-start(), calls=%async_computation | async-start | bytes 524288 | tf_op jit(solution)/shard_map/while/body/eval_jaxpr/psum | solution.py:12
  922.1 206.5 %all-gather.3.cloned.1.call-start = ((), (), s32[]{:S(2)}) async-start(), calls=%async_computation.1 | async-start | bytes 8912896 | tf_op jit(solution)/shard_map/while/body/eval_jaxpr/all_gather | solution.py:57
  1008.2 27.0 %copy-start.2 = (f32[256,256]{0,1:T(8,128)S(1)}, f32[256,256]{0,1:T(8,128)}, u32[]{:S(2)}) copy-start(f32[256,256]{0,1:T(8,128)} %all-reduce.3.cloned.1.call-done) | copy-start | bytes 786436 | tf_op jit(solution)/shard_map/while
  1144.1 9.7 copy-start
  1159.5 2.0 copy-start.1
  1161.5 5.6 copy-start.3
  1161.5 5.6 copy-start.5
  1161.5 23.1 %copy-start.8 = (f32[16,16]{1,0:T(8,128)S(1)}, f32[16,16]{1,0:T(8,128)}, u32[]{:S(2)}) copy-start(f32[16,16]{1,0:T(8,128)} %param.17) | copy-start | bytes 3076
Sparse Core Ops, SparseCore 0:
  84.7 91.3 all-reduce.2
  204.2 79.6 all-gather.2
  367.6 85.8 all-reduce.2
  481.6 79.6 all-gather.2
  644.9 85.8 all-reduce.2
  758.9 79.6 all-gather.2
  922.3 85.8 all-reduce.2
  1036.3 79.6 all-gather.2
